TPU v7x, 256 devices: a whole 4x4x8 slice. The times are simulated.
256 devices in a mesh: tm: 16 (over z, core), tile: 16 (over x, y).
Axes of the slice: x: 4, y: 4, z: 8, core: 2. Of those that a mesh axis runs over, the one named last changes fastest.
Arguments:
- obs_values: bfloat16 [16, 32768, 128], P('tm', 'tile'), may hold values from -6 to 6
- obs_weight: bfloat16 [16, 32768, 128], P('tm', 'tile'), may hold values from 0.19921875 to 2
- obs_count: int32 [16, 32768], P('tm', 'tile'), may hold values from 32 to 128
- dest_tile: int32 [16, 32768, 1], P('tm', 'tile'), may hold values from 0 to 15; in each aligned block of 2048 rows (0 to 2047, 2048 to 4095, ..., all dimensions but the last counted through in order) at most 256 rows name the same one
- jac_index: int32 [16, 32768], P('tm', 'tile'), may hold values from 0 to 255
- jacobian: bfloat16 [16, 4096, 128, 128], P('tm', 'tile'), may hold values from -0.5 to 0.5
- jac_state: int32 [16, 4096], P('tm', 'tile'), may hold values from 0 to 63
- corr_blocks: bfloat16 [16, 768, 128, 128], P('tm', 'tile'), may hold values from -0.625 to 0.625
- corr_row: int32 [16, 768], P('tm', 'tile'), may hold values from 0 to 63
- corr_col: int32 [16, 768], P('tm', 'tile'), may hold values from 0 to 63
- time_coupling: bfloat16 [16, 1024, 128], P('tm', 'tile'), may hold values from 0.19921875 to 0.59765625
Outputs:
- product: bfloat16 [16, 32768, 128], P('tm', 'tile')
Inputs may be any that keep to these rules, and one draw needn't show every extreme that they name: `dest_tile`: in the rows of one device, no tile is named by more than 256 observation blocks, a bound that some block reaches.
All inputs are finite; a program needn't handle non-finite values.
Results may differ from a plain program's by a relative error of at most 0.0075.
Values may be sent and summed in bfloat16 or wider, within the bound.
No kernel may reach another device: no remote copies, remote signals or barrier semaphores. Data moves between devices by JAX's collectives and lax.ppermute only.
A program may use at most 64 MiB of HBM per device.

v0:
```python
import jax
import jax.numpy as jnp
from jax import lax
from jax.sharding import PartitionSpec as P


def from_behind(x, axis, by):
    length = lax.axis_size(axis)
    pairs = [(i, i + by) for i in range(length) if 0 <= i + by < length]
    return lax.ppermute(x, axis, pairs)


def shards(
    obs_values,
    obs_weight,
    obs_count,
    dest_tile,
    jac_index,
    jacobian,
    jac_state,
    corr_blocks,
    corr_row,
    corr_col,
    time_coupling,
):
    obs_total = obs_values.shape[1]
    block_width = obs_values.shape[2]
    jac_total = jacobian.shape[1]
    state_total = time_coupling.shape[1]
    lane_index = lax.broadcasted_iota(jnp.int32, (obs_total, block_width), 1)
    keeping = (lane_index < obs_count[0][:, None]).astype(jnp.float32)
    weighted = (
        obs_values[0].astype(jnp.float32) * obs_weight[0].astype(jnp.float32) * keeping
    ).astype(jnp.bfloat16)
    target = dest_tile[0, :, 0]
    column = jac_index[0]
    bin_id = target * jac_total + column
    row_ids = lax.broadcasted_iota(jnp.int32, (jac_total * lax.axis_size("tile"), obs_total), 0)
    picker = (row_ids == bin_id[None, :]).astype(jnp.bfloat16)
    summed = lax.psum_scatter(
        jnp.dot(picker, weighted, preferred_element_type=jnp.float32),
        "tile",
        scatter_dimension=0,
        tiled=True,
    )
    merged = summed.astype(jnp.bfloat16)
    spread = jnp.einsum("kij,ki->kj", jacobian[0], merged, preferred_element_type=jnp.float32)
    state_ids = lax.broadcasted_iota(jnp.int32, (state_total, jac_total), 0)
    owners = state_ids == jac_state[0][None, :]
    state = jnp.dot(owners.astype(jnp.float32), spread, precision=lax.Precision.HIGHEST).astype(
        jnp.bfloat16
    )
    corr_total = corr_blocks.shape[1]
    read_ids = lax.broadcasted_iota(jnp.int32, (corr_total, state_total), 1)
    reader = (read_ids == corr_col[0][:, None]).astype(jnp.bfloat16)
    source = jnp.dot(reader, state, preferred_element_type=jnp.float32).astype(jnp.bfloat16)
    mixing = jnp.einsum("cij,cj->ci", corr_blocks[0], source, preferred_element_type=jnp.float32)
    write_ids = lax.broadcasted_iota(jnp.int32, (state_total, corr_total), 0)
    writer = (write_ids == corr_row[0][None, :]).astype(jnp.float32)
    spatial = jnp.dot(writer, mixing, precision=lax.Precision.HIGHEST).astype(jnp.bfloat16)
    coupling = time_coupling[0]
    earlier = from_behind(spatial, "tm", 1)
    later_state, later_coupling = from_behind((spatial, coupling), "tm", -1)
    coupled = (
        spatial.astype(jnp.float32)
        + coupling.astype(jnp.float32) * earlier.astype(jnp.float32)
        + later_coupling.astype(jnp.float32) * later_state.astype(jnp.float32)
    ).astype(jnp.bfloat16)
    local_state = jnp.dot(
        owners.T.astype(jnp.bfloat16), coupled, preferred_element_type=jnp.float32
    ).astype(jnp.bfloat16)
    model_obs = jnp.einsum(
        "kij,kj->ki", jacobian[0], local_state, preferred_element_type=jnp.float32
    ).astype(jnp.bfloat16)
    portion = lax.all_gather(model_obs, "tile", axis=0, tiled=True)
    columns = lax.broadcasted_iota(jnp.int32, (obs_total, portion.shape[0]), 1)
    picker = (bin_id[:, None] == columns).astype(jnp.bfloat16)
    gathered = jnp.dot(picker, portion, preferred_element_type=jnp.float32)
    return (gathered * keeping).astype(jnp.bfloat16)[None]


def solution(mesh):
    in_specs = (
        P("tm", "tile", None),
        P("tm", "tile", None),
        P("tm", "tile"),
        P("tm", "tile", None),
        P("tm", "tile"),
        P("tm", "tile", None, None),
        P("tm", "tile"),
        P("tm", "tile", None, None),
        P("tm", "tile"),
        P("tm", "tile"),
        P("tm", "tile", None),
    )
    out_specs = P("tm", "tile", None)
    return jax.shard_map(shards, mesh=mesh, in_specs=in_specs, out_specs=out_specs, check_vma=False)
```

profile of v0, /device:TPU:2, one launch (start us, length us, event | category | flops | bytes accessed | tf_op | source)
XLA Modules:
  0.0 185.7 jit_solution(13283383729035749452)
XLA Ops:
  6.5 0.0 copy-start
  6.5 0.0 reduce-scatter.2.cloned.1.call-start
  6.5 0.8 bitcast_add_fusion
  7.4 0.0 copy-start.3
  7.4 8.6 %fusion = f32[4096,128]{1,0:T(8,128)} fusion(s32[2048]{0:T(1024)S(1)} %bitcast.51, bf16[1,2048,128]{2,1,0:T(8,128)(2,1)} %param.12, bf16[1,2048,128]{2,1,0:T(8,128)(2,1)} %param.11, s32[2048]{0:T(1024)} %bitcast.55), kind=kOutput, calls=%fused_computation.2 | convolution fusion | flops 2157445120 | bytes 3162112 | tf_op jit(solution)/shard_map/dot_general | solution.py:41
  16.0 0.0 copy-start.4
  16.0 0.0 copy-start.7
  16.0 0.0 copy-start.5
  16.0 0.0 reduce-scatter.2.cloned.1.call-update
  16.0 0.0 all-gather.2.cloned.1.call-start
  16.1 0.0 copy-done.3
  16.1 1.3 collective-permute-start.1
  17.4 81.6 %reduce-scatter.2.cloned.1.call-done = f32[256,128]{1,0:T(8,128)} async-done(((f32[4096,128]{1,0:T(8,128)}), f32[256,128]{1,0:T(8,128)}) %reduce-scatter.2.cloned.1.call-update) | async-done | bytes 131088 | tf_op jit(solution)/shard_map/reduce_scatter | solution.py:40
  99.0 0.9 convert_bitcast_fusion
  99.9 0.0 copy-start.2
  99.9 0.0 copy-start.1
  99.9 0.0 copy-start.6
  99.9 5.7 %fusion.6 = f32[256,1,128]{2,1,0:T(1,128)S(1)} fusion(bf16[1,256,128,128]{3,2,1,0:T(8,128)(2,1)} %param.16, bf16[256,128,1]{1,0,2:T(8,128)(2,1)S(1)} %convert_bitcast_fusion), kind=kOutput, calls=%fused_computation.8 | convolution fusion | flops 8388608 | bytes 8585216 | tf_op jit(solution)/shard_map/kij,ki->kj/dot_general | solution.py:47
  105.6 0.0 copy-done.4
  105.6 0.2 convolution_convert_fusion.2
  105.8 0.0 copy-done.7
  105.8 0.2 fusion.14
  106.0 0.0 copy-done
  106.0 0.9 fusion.11
  106.9 0.0 copy-done.5
  106.9 0.2 convolution_convert_fusion.1
  107.1 1.3 collective-permute-start
  108.4 1.5 collective-permute-start.2
  109.9 0.0 collective-permute-done.1
  109.9 0.0 collective-permute-done
  109.9 3.4 %collective-permute-done.2 = bf16[64,128]{1,0:T(8,128)(2,1)S(1)} collective-permute-done((bf16[64,128]{1,0:T(8,128)(2,1)S(1)}, bf16[64,128]{1,0:T(8,128)(2,1)S(1)}, u32[]{:S(2)}, u32[]{:S(2)}) %collective-permute-start.2) | collective-permute-done | bytes 16416 | tf_op jit(solution)/shard_map/ppermute | solution.py:10
  113.3 0.2 fusion.13
  113.5 7.8 %fusion.4 = f32[256,1,128]{2,1,0:T(1,128)S(1)} fusion(bf16[1,256,128,128]{3,2,1,0:T(8,128)(2,1)} %param.16, bf16[256,128,1]{1,0,2:T(8,128)(2,1)S(1)} %fusion.13), kind=kOutput, calls=%fused_computation.6 | convolution fusion | flops 8388608 | bytes 8585216 | tf_op jit(solution)/shard_map/kij,kj->ki/dot_general | solution.py:72
  121.3 0.7 convert_element_type.71
  121.9 0.0 all-gather.2.cloned.1.call-update
  121.9 0.0 copy-done.2
  122.0 0.0 copy-done.1
  122.0 49.3 %all-gather.2.cloned.1.call-done = bf16[4096,128]{1,0:T(8,128)(2,1)} async-done(((bf16[256,128]{1,0:T(8,128)(2,1)}), bf16[4096,128]{1,0:T(8,128)(2,1)}) %all-gather.2.cloned.1.call-update) | async-done | bytes 1048592 | tf_op jit(solution)/shard_map/all_gather | solution.py:75
  171.3 0.0 copy-done.6
  171.3 7.6 %fusion.10 = bf16[1,2048,128]{2,1,0:T(8,128)(2,1)} fusion(bf16[4096,128]{1,0:T(8,128)(2,1)} %all-gather.2.cloned.1.call-done, s32[2048]{0:T(1024)S(1)} %add.18, s32[2048]{0:T(1024)S(1)} %bitcast.56), kind=kOutput, calls=%fused_computation.12 | convolution fusion | flops 2156658688 | bytes 1589248 | tf_op jit(solution)/shard_map/dot_general | solution.py:78
  (2 shorter events, 0.0 us)
Async XLA Ops:
  6.5 99.5 %copy-start = (bf16[1,48,128,128]{3,2,1,0:T(8,128)(2,1)S(1)}, bf16[1,48,128,128]{3,2,1,0:T(8,128)(2,1)}, u32[]{:S(2)}) copy-start(bf16[1,48,128,128]{3,2,1,0:T(8,128)(2,1)} %param.18) | copy-start | bytes 4718596
  6.5 92.5 %reduce-scatter.2.cloned.1.call-start = ((), (), s32[]{:S(2)}) async-start(), calls=%async_computation.1 | async-start | bytes 2228224 | tf_op jit(solution)/shard_map/reduce_scatter | solution.py:40
  7.4 8.7 %copy-start.3 = (bf16[1,64,128]{2,1,0:T(8,128)(2,1)S(1)}, bf16[1,64,128]{2,1,0:T(8,128)(2,1)}, u32[]{:S(2)}) copy-start(bf16[1,64,128]{2,1,0:T(8,128)(2,1)} %param.21) | copy-start | bytes 49156
  16.0 89.6 %copy-start.4 = (s32[1,256]{1,0:T(1,128)S(1)}, s32[1,256]{1,0:T(1,128)}, u32[]{:S(2)}) copy-start(s32[1,256]{1,0:T(1,128)} %param.17) | copy-start | bytes 3076
  16.0 89.8 %copy-start.7 = (s32[1,48]{1,0:T(1,128)S(1)}, s32[1,48]{1,0:T(1,128)}, u32[]{:S(2)}) copy-start(s32[1,48]{1,0:T(1,128)} %param.20) | copy-start | bytes 580
  16.0 90.9 %copy-start.5 = (s32[1,48]{1,0:T(1,128)S(1)}, s32[1,48]{1,0:T(1,128)}, u32[]{:S(2)}) copy-start(s32[1,48]{1,0:T(1,128)} %param.19) | copy-start | bytes 580
  16.0 155.3 %all-gather.2.cloned.1.call-start = ((), (), s32[]{:S(2)}) async-start(), calls=%async_computation.2 | async-start | bytes 1114112 | tf_op jit(solution)/shard_map/all_gather | solution.py:75
  16.1 93.8 %collective-permute-start.1 = (bf16[64,128]{1,0:T(8,128)(2,1)S(1)}, bf16[64,128]{1,0:T(8,128)(2,1)S(1)}, u32[]{:S(2)}, u32[]{:S(2)}) collective-permute-start(bf16[64,128]{1,0:T(8,128)(2,1)S(1)} %bitcast.50), channel_id=1, source_target_pairs={{16,0},{32,16},{48,32},{64,48},{80,64},{96,80},{112,96},{128,112},... | collective-permute-start | bytes 49160 | tf_op jit(solution)/shard_map/ppermute | solution.py:10
  99.9 22.0 %copy-start.2 = (s32[1,2048,1]{1,2,0:T(1,128)S(1)}, s32[1,2048,1]{1,2,0:T(1,128)}, u32[]{:S(2)}) copy-start(s32[1,2048,1]{1,2,0:T(1,128)} %param.14) | copy-start | bytes 24580
  99.9 22.1 %copy-start.1 = (s32[1,2048]{1,0:T(1,128)S(1)}, s32[1,2048]{1,0:T(1,128)}, u32[]{:S(2)}) copy-start(s32[1,2048]{1,0:T(1,128)} %param.15) | copy-start | bytes 24580
  99.9 71.4 %copy-start.6 = (s32[1,2048]{1,0:T(1,128)S(1)}, s32[1,2048]{1,0:T(1,128)}, u32[]{:S(2)}) copy-start(s32[1,2048]{1,0:T(1,128)} %param.13) | copy-start | bytes 24580
  107.1 2.8 %collective-permute-start = (bf16[64,128]{1,0:T(8,128)(2,1)S(1)}, bf16[64,128]{1,0:T(8,128)(2,1)S(1)}, u32[]{:S(2)}, u32[]{:S(2)}) collective-permute-start(bf16[64,128]{1,0:T(8,128)(2,1)S(1)} %convolution_convert_fusion.1), channel_id=1, source_target_pairs={{0,16},{16,32},{32,48},{48,64},{64,80},{80,96},{96,112},{112,128},... | collective-permute-start | bytes 49160 | tf_op jit(solution)/shard_map/ppermute | solution.py:10
  108.4 4.9 %collective-permute-start.2 = (bf16[64,128]{1,0:T(8,128)(2,1)S(1)}, bf16[64,128]{1,0:T(8,128)(2,1)S(1)}, u32[]{:S(2)}, u32[]{:S(2)}) collective-permute-start(bf16[64,128]{1,0:T(8,128)(2,1)S(1)} %convolution_convert_fusion.1), channel_id=1, source_target_pairs={{16,0},{32,16},{48,32},{64,48},{80,64},{96,80},{112,96},{128,112},... | collective-permute-start | bytes 49160 | tf_op jit(solution)/shard_map/ppermute | solution.py:10
Sparse Core Ops, SparseCore 0:
  16.1 82.8 reduce-scatter.1
  122.1 49.1 all-gather.1
where the time goes:
time: 186 us
  waiting for transfers between devices  134 us (72%)
  matrix products  31.3 us (17%)
  between operations  13.5 us (7%)
  starting transfers between devices  4.1 us (2%)
  other arithmetic  2.44 us (1%)
    reduce_scatter x1, waiting for transfers between devices, shards(): lax.psum_scatter(jnp.dot(picker, weighted, preferred_element_type=jnp.flo...  81.6 us
    all_gather x1, waiting for transfers between devices, shards(): portion = lax.all_gather(model_obs, 'tile', axis=0, tiled=True)  49.3 us
    dot_general x1, matrix products, shards(): jnp.dot(picker, weighted, preferred_element_type=jnp.float32)  8.59 us
    dot_general x1, matrix products, shards(): jnp.einsum('kij,kj->ki', jacobian[0], local_state, preferred_element_type...  7.78 us
    dot_general x1, matrix products, shards(): gathered = jnp.dot(picker, portion, preferred_element_type=jnp.float32)  7.57 us
    dot_general x1, matrix products, shards(): jnp.einsum('kij,ki->kj', jacobian[0], merged, preferred_element_type=jnp....  5.66 us
    ppermute x3, starting transfers between devices, from_behind(): return lax.ppermute(x, axis, pairs)  4.06 us
  transfers between devices with their start and end apart: 5, of which 3 were waited for; matrix products, arithmetic and copies ran while one was open for 4% of the time, Pallas kernels for 0%

commit v1 on v0

--- a/solution.py
+++ b/solution.py
@@ -72,7 +72,9 @@
     model_obs = jnp.einsum(
         "kij,kj->ki", jacobian[0], local_state, preferred_element_type=jnp.float32
     ).astype(jnp.bfloat16)
-    portion = lax.all_gather(model_obs, "tile", axis=0, tiled=True)
+    portion = jnp.concatenate(
+        lax.all_to_all(jnp.stack([model_obs] * lax.axis_size("tile")), "tile", 0, 0), axis=0
+    )
     columns = lax.broadcasted_iota(jnp.int32, (obs_total, portion.shape[0]), 1)
     picker = (bin_id[:, None] == columns).astype(jnp.bfloat16)
     gathered = jnp.dot(picker, portion, preferred_element_type=jnp.float32)

time: 186 us -> 162 us (0.87)
  the two profiles are of different devices: /device:TPU:2 before, /device:TPU:1 now
where the time goes in v1:
time: 162 us
  waiting for transfers between devices  97.1 us (60%)
  matrix products  30.7 us (19%)
  starting transfers between devices  17.2 us (11%)
  between operations  13.5 us (8%)
  other arithmetic  1.8 us (1%)
    reduce_scatter x1, waiting for transfers between devices, shards(): lax.psum_scatter(jnp.dot(picker, weighted, preferred_element_type=jnp.flo...  77.2 us
    all_to_all x1, waiting for transfers between devices, shards(): lax.all_to_all(jnp.stack([model_obs] * lax.axis_size('tile')), 'tile', 0, 0)  16.8 us
    ppermute x3, starting transfers between devices, from_behind(): return lax.ppermute(x, axis, pairs)  12.6 us
    dot_general x1, matrix products, shards(): jnp.dot(picker, weighted, preferred_element_type=jnp.float32)  8.58 us
    dot_general x1, matrix products, shards(): jnp.einsum('kij,kj->ki', jacobian[0], local_state, preferred_element_type...  7.78 us
    dot_general x1, matrix products, shards(): gathered = jnp.dot(picker, portion, preferred_element_type=jnp.float32)  6.99 us
    dot_general x1, matrix products, shards(): jnp.einsum('kij,ki->kj', jacobian[0], merged, preferred_element_type=jnp....  5.65 us
    all_to_all x1, starting transfers between devices, shards(): lax.all_to_all(jnp.stack([model_obs] * lax.axis_size('tile')), 'tile', 0, 0)  4.66 us
  transfers between devices with their start and end apart: 5, of which 3 were waited for; matrix products, arithmetic and copies ran while one was open for 5% of the time, Pallas kernels for 0%

profile of v1, /device:TPU:1, one launch (start us, length us, event | category | flops | bytes accessed | tf_op | source)
XLA Modules:
  0.0 161.5 jit_solution(11691634229986752999)
XLA Ops:
  6.5 0.0 copy-start
  6.5 0.0 reduce-scatter.2.cloned.1.call-start
  6.5 0.8 bitcast_add_fusion
  7.4 0.0 copy-start.3
  7.4 8.6 %fusion = f32[4096,128]{1,0:T(8,128)} fusion(s32[2048]{0:T(1024)S(1)} %bitcast.53, bf16[1,2048,128]{2,1,0:T(8,128)(2,1)} %param.12, bf16[1,2048,128]{2,1,0:T(8,128)(2,1)} %param.11, s32[2048]{0:T(1024)} %bitcast.57), kind=kOutput, calls=%fused_computation.2 | convolution fusion | flops 2157445120 | bytes 3162112 | tf_op jit(solution)/shard_map/dot_general | solution.py:41
  16.0 0.0 copy-start.4
  16.0 0.0 copy-start.7
  16.0 0.0 copy-start.5
  16.0 0.0 reduce-scatter.2.cloned.1.call-update
  16.0 0.0 copy-done.3
  16.0 5.2 %collective-permute-start.1 = (bf16[64,128]{1,0:T(8,128)(2,1)S(1)}, bf16[64,128]{1,0:T(8,128)(2,1)S(1)}, u32[]{:S(2)}, u32[]{:S(2)}) collective-permute-start(bf16[64,128]{1,0:T(8,128)(2,1)S(1)} %bitcast.52), channel_id=1, source_target_pairs={{16,0},{32,16},{48,32},{64,48},{80,64},{96,80},{112,96},{128,112},... | collective-permute-start | bytes 49160 | tf_op jit(solution)/shard_map/ppermute | solution.py:10
  21.3 77.2 %reduce-scatter.2.cloned.1.call-done = f32[256,128]{1,0:T(8,128)} async-done(((f32[4096,128]{1,0:T(8,128)}), f32[256,128]{1,0:T(8,128)}) %reduce-scatter.2.cloned.1.call-update) | async-done | bytes 131088 | tf_op jit(solution)/shard_map/reduce_scatter | solution.py:40
  98.4 0.9 convert_bitcast_fusion
  99.4 5.6 %fusion.6 = f32[256,1,128]{2,1,0:T(1,128)S(1)} fusion(bf16[1,256,128,128]{3,2,1,0:T(8,128)(2,1)} %param.16, bf16[256,128,1]{1,0,2:T(8,128)(2,1)S(1)} %convert_bitcast_fusion), kind=kOutput, calls=%fused_computation.8 | convolution fusion | flops 8388608 | bytes 8585216 | tf_op jit(solution)/shard_map/kij,ki->kj/dot_general | solution.py:47
  105.0 0.0 copy-start.2
  105.0 0.0 copy-start.1
  105.0 0.0 copy-start.6
  105.0 0.0 copy-done.4
  105.0 0.2 convolution_convert_fusion.2
  105.2 0.0 copy-done.7
  105.2 0.2 fusion.14
  105.4 0.0 copy-done
  105.4 0.9 fusion.11
  106.3 0.0 copy-done.5
  106.3 0.2 convolution_convert_fusion.1
  106.5 5.4 %collective-permute-start = (bf16[64,128]{1,0:T(8,128)(2,1)S(1)}, bf16[64,128]{1,0:T(8,128)(2,1)S(1)}, u32[]{:S(2)}, u32[]{:S(2)}) collective-permute-start(bf16[64,128]{1,0:T(8,128)(2,1)S(1)} %convolution_convert_fusion.1), channel_id=1, source_target_pairs={{0,16},{16,32},{32,48},{48,64},{64,80},{80,96},{96,112},{112,128},... | collective-permute-start | bytes 49160 | tf_op jit(solution)/shard_map/ppermute | solution.py:10
  111.9 1.9 %collective-permute-start.2 = (bf16[64,128]{1,0:T(8,128)(2,1)S(1)}, bf16[64,128]{1,0:T(8,128)(2,1)S(1)}, u32[]{:S(2)}, u32[]{:S(2)}) collective-permute-start(bf16[64,128]{1,0:T(8,128)(2,1)S(1)} %convolution_convert_fusion.1), channel_id=1, source_target_pairs={{16,0},{32,16},{48,32},{64,48},{80,64},{96,80},{112,96},{128,112},... | collective-permute-start | bytes 49160 | tf_op jit(solution)/shard_map/ppermute | solution.py:10
  113.8 0.0 collective-permute-done.1
  113.9 0.0 collective-permute-done
  113.9 3.1 %collective-permute-done.2 = bf16[64,128]{1,0:T(8,128)(2,1)S(1)} collective-permute-done((bf16[64,128]{1,0:T(8,128)(2,1)S(1)}, bf16[64,128]{1,0:T(8,128)(2,1)S(1)}, u32[]{:S(2)}, u32[]{:S(2)}) %collective-permute-start.2) | collective-permute-done | bytes 16416 | tf_op jit(solution)/shard_map/ppermute | solution.py:10
  117.0 0.2 fusion.13
  117.2 7.8 %fusion.4 = f32[256,1,128]{2,1,0:T(1,128)S(1)} fusion(bf16[1,256,128,128]{3,2,1,0:T(8,128)(2,1)} %param.16, bf16[256,128,1]{1,0,2:T(8,128)(2,1)S(1)} %fusion.13), kind=kOutput, calls=%fused_computation.6 | convolution fusion | flops 8388608 | bytes 8585216 | tf_op jit(solution)/shard_map/kij,kj->ki/dot_general | solution.py:72
  125.0 1.2 stack.2
  126.2 4.7 %all-to-all-start = ((bf16[16,256,128]{2,1,0:T(8,128)(2,1)}), bf16[16,256,128]{2,1,0:T(8,128)(2,1)S(1)}, u32[]{:S(2)}, u32[]{:S(2)}) async-start(bf16[16,256,128]{2,1,0:T(8,128)(2,1)} %stack.2), calls=%async_computation.1 | async-start | bytes 2097152 | tf_op jit(solution)/shard_map/all_to_all | solution.py:76
  130.9 0.0 copy-done.2
  130.9 0.0 copy-done.1
  130.9 16.8 %all-to-all-done = bf16[16,256,128]{2,1,0:T(8,128)(2,1)S(1)} async-done(((bf16[16,256,128]{2,1,0:T(8,128)(2,1)}), bf16[16,256,128]{2,1,0:T(8,128)(2,1)S(1)}, u32[]{:S(2)}, u32[]{:S(2)}) %all-to-all-start) | async-done | bytes 1048608 | tf_op jit(solution)/shard_map/all_to_all | solution.py:76
  147.7 0.0 copy-done.6
  147.7 7.0 %fusion.10 = bf16[1,2048,128]{2,1,0:T(8,128)(2,1)} fusion(bf16[4096,128]{1,0:T(8,128)(2,1)S(1)} %bitcast.46, s32[2048]{0:T(1024)S(1)} %add.18, s32[2048]{0:T(1024)S(1)} %bitcast.58), kind=kOutput, calls=%fused_computation.12 | convolution fusion | flops 2156658688 | bytes 1589248 | tf_op jit(solution)/shard_map/dot_general | solution.py:80
  (3 shorter events, 0.0 us)
Async XLA Ops:
  6.5 98.9 %copy-start = (bf16[1,48,128,128]{3,2,1,0:T(8,128)(2,1)S(1)}, bf16[1,48,128,128]{3,2,1,0:T(8,128)(2,1)}, u32[]{:S(2)}) copy-start(bf16[1,48,128,128]{3,2,1,0:T(8,128)(2,1)} %param.18) | copy-start | bytes 4718596
  6.5 91.9 %reduce-scatter.2.cloned.1.call-start = ((), (), s32[]{:S(2)}) async-start(), calls=%async_computation.2 | async-start | bytes 2228224 | tf_op jit(solution)/shard_map/reduce_scatter | solution.py:40
  7.4 8.6 %copy-start.3 = (bf16[1,64,128]{2,1,0:T(8,128)(2,1)S(1)}, bf16[1,64,128]{2,1,0:T(8,128)(2,1)}, u32[]{:S(2)}) copy-start(bf16[1,64,128]{2,1,0:T(8,128)(2,1)} %param.21) | copy-start | bytes 49156
  16.0 89.0 %copy-start.4 = (s32[1,256]{1,0:T(1,128)S(1)}, s32[1,256]{1,0:T(1,128)}, u32[]{:S(2)}) copy-start(s32[1,256]{1,0:T(1,128)} %param.17) | copy-start | bytes 3076
  16.0 89.2 %copy-start.7 = (s32[1,48]{1,0:T(1,128)S(1)}, s32[1,48]{1,0:T(1,128)}, u32[]{:S(2)}) copy-start(s32[1,48]{1,0:T(1,128)} %param.20) | copy-start | bytes 580
  16.0 90.4 %copy-start.5 = (s32[1,48]{1,0:T(1,128)S(1)}, s32[1,48]{1,0:T(1,128)}, u32[]{:S(2)}) copy-start(s32[1,48]{1,0:T(1,128)} %param.19) | copy-start | bytes 580
  16.0 97.8 %collective-permute-start.1 = (bf16[64,128]{1,0:T(8,128)(2,1)S(1)}, bf16[64,128]{1,0:T(8,128)(2,1)S(1)}, u32[]{:S(2)}, u32[]{:S(2)}) collective-permute-start(bf16[64,128]{1,0:T(8,128)(2,1)S(1)} %bitcast.52), channel_id=1, source_target_pairs={{16,0},{32,16},{48,32},{64,48},{80,64},{96,80},{112,96},{128,112},... | collective-permute-start | bytes 49160 | tf_op jit(solution)/shard_map/ppermute | solution.py:10
  105.0 25.8 %copy-start.2 = (s32[1,2048,1]{1,2,0:T(1,128)S(1)}, s32[1,2048,1]{1,2,0:T(1,128)}, u32[]{:S(2)}) copy-start(s32[1,2048,1]{1,2,0:T(1,128)} %param.14) | copy-start | bytes 24580
  105.0 25.9 %copy-start.1 = (s32[1,2048]{1,0:T(1,128)S(1)}, s32[1,2048]{1,0:T(1,128)}, u32[]{:S(2)}) copy-start(s32[1,2048]{1,0:T(1,128)} %param.15) | copy-start | bytes 24580
  105.0 42.7 %copy-start.6 = (s32[1,2048]{1,0:T(1,128)S(1)}, s32[1,2048]{1,0:T(1,128)}, u32[]{:S(2)}) copy-start(s32[1,2048]{1,0:T(1,128)} %param.13) | copy-start | bytes 24580
  106.5 7.3 %collective-permute-start = (bf16[64,128]{1,0:T(8,128)(2,1)S(1)}, bf16[64,128]{1,0:T(8,128)(2,1)S(1)}, u32[]{:S(2)}, u32[]{:S(2)}) collective-permute-start(bf16[64,128]{1,0:T(8,128)(2,1)S(1)} %convolution_convert_fusion.1), channel_id=1, source_target_pairs={{0,16},{16,32},{32,48},{48,64},{64,80},{80,96},{96,112},{112,128},... | collective-permute-start | bytes 49160 | tf_op jit(solution)/shard_map/ppermute | solution.py:10
  111.9 5.1 %collective-permute-start.2 = (bf16[64,128]{1,0:T(8,128)(2,1)S(1)}, bf16[64,128]{1,0:T(8,128)(2,1)S(1)}, u32[]{:S(2)}, u32[]{:S(2)}) collective-permute-start(bf16[64,128]{1,0:T(8,128)(2,1)S(1)} %convolution_convert_fusion.1), channel_id=1, source_target_pairs={{16,0},{32,16},{48,32},{64,48},{80,64},{96,80},{112,96},{128,112},... | collective-permute-start | bytes 49160 | tf_op jit(solution)/shard_map/ppermute | solution.py:10
  126.2 21.5 %all-to-all-start = ((bf16[16,256,128]{2,1,0:T(8,128)(2,1)}), bf16[16,256,128]{2,1,0:T(8,128)(2,1)S(1)}, u32[]{:S(2)}, u32[]{:S(2)}) async-start(bf16[16,256,128]{2,1,0:T(8,128)(2,1)} %stack.2), calls=%async_computation.1 | async-start | bytes 2097152 | tf_op jit(solution)/shard_map/all_to_all | solution.py:76
Sparse Core Ops, SparseCore 0:
  16.1 82.2 reduce-scatter.1
